TPU v7x, 128 devices: a whole 4x4x4 slice. The times are simulated.
128 devices in a mesh: row: 8 (over y, core), col: 16 (over z, x).
Axes of the slice: x: 4, y: 4, z: 4, core: 2. Of those that a mesh axis runs over, the one named last changes fastest.
Arguments:
- fock: bfloat16 [32768, 16, 2048], P('row', 'col'), may hold values from -6 to 6
- lmo_coef: bfloat16 [32768, 1024], P(('row', 'col')), may hold values from -0.078125 to 0.078125
- three_index: bfloat16 [32768, 512], P(('row', 'col')), may hold values from -6 to 6
- rotation: bfloat16 [16, 8, 1024, 512], P('col', 'row'), may hold values from -0.1875 to 0.1875
- lmo_ids: int32 [16, 8], replicated, may hold values from 0 to 127, as said below
- domains: int32 [128, 8], replicated, may hold values from -1 to 255, as said below
Outputs:
- proj_fock: float32 [16, 8, 512, 512], P('col', 'row')
- three_rot: bfloat16 [16, 8, 512, 512], P('col', 'row')
Inputs may be any that keep to these rules, and one draw needn't show every extreme that they name: `lmo_ids`: every LMO number appears exactly once; row o lists the 8 LMOs owned by column set o. `domains`: entry k of a list is -1 or a block of row panel k; entry 0 is never -1. The present blocks of one list lie in distinct column sets. For one owner o and one entry k, the blocks of the lists of lmo_ids[o, j] over all j lie in distinct column sets; for one j and one entry k, those of lmo_ids[o, j] over all o do too.
All inputs are finite; a program needn't handle non-finite values.
Results may differ from a plain program's by a relative error of at most 0.02.
Values may be sent and summed in bfloat16 or wider, within the bound.
No kernel may reach another device: no remote copies, remote signals or barrier semaphores. Data moves between devices by JAX's collectives and lax.ppermute only.
A program may use at most 192 MiB of HBM per device.

v0:
```python
import jax
import jax.numpy as jnp
from jax import lax
from jax.sharding import PartitionSpec as P

BLK = 128


def locate(blocks, dev_blocks, num_sets):
    present = blocks >= 0
    clipped = jnp.maximum(blocks, 0)
    flat_dev = clipped // dev_blocks
    return (present, flat_dev % num_sets, flat_dev // num_sets, clipped % dev_blocks)


def body(fock, lmo_coef, three_index, rotation, lmo_ids, domains):
    num_panels = lax.axis_size("row")
    num_sets = lax.axis_size("col")
    my_row = lax.axis_index("row")
    my_col = lax.axis_index("col")
    dev_rows = lmo_coef.shape[0]
    occ_width = lmo_coef.shape[1]
    dev_blocks = dev_rows // BLK
    dom_blocks = domains.shape[1]
    per_panel = dom_blocks // num_panels
    dev_lmos = rotation.shape[1]
    dom_width = dom_blocks * BLK
    panel_fock = fock[:, 0, :]
    gathered = lax.all_gather(lmo_coef, "row", axis=0, tiled=True)
    fock_coef = lax.psum_scatter(
        jnp.dot(panel_fock, gathered, preferred_element_type=jnp.float32).astype(jnp.bfloat16),
        "col",
        scatter_dimension=0,
        tiled=True,
    ).astype(jnp.float32)
    occ_term = jnp.einsum(
        "ri,rj->ij", lmo_coef, fock_coef.astype(jnp.bfloat16), preferred_element_type=jnp.float32
    )
    occ_fock = lax.psum(occ_term, ("row", "col"))
    correction = jnp.dot(
        lmo_coef, occ_fock.astype(jnp.bfloat16), preferred_element_type=jnp.float32
    )
    proj_rows = (fock_coef - 0.5 * correction).astype(jnp.bfloat16)
    all_rows = jnp.concatenate([lmo_coef, proj_rows, three_index], axis=1)
    row_width = all_rows.shape[1]
    row_blocks = all_rows.reshape(dev_blocks, BLK, row_width)
    fock_tiles = panel_fock.reshape(num_sets * dev_blocks, BLK, num_panels * dev_blocks, BLK)
    owner_doms = jnp.take(domains, lmo_ids, axis=0)
    present, col_set, panel_id, sub_block = locate(owner_doms, dev_blocks, num_sets)
    row_tile = col_set * dev_blocks + sub_block
    col_tile = panel_id * dev_blocks + sub_block
    holds_col = present & (col_set == my_col)
    my_col_tile = jnp.sum(jnp.where(holds_col, col_tile, 0), axis=2)
    has_col = jnp.any(holds_col, axis=2)
    sub_range = jnp.arange(dev_blocks, dtype=jnp.int32)
    set_range = jnp.arange(num_sets, dtype=jnp.int32)
    slot_start = my_row * per_panel
    mine_slot = lax.dynamic_slice_in_dim(holds_col, slot_start, per_panel, 2)
    sub_slot = lax.dynamic_slice_in_dim(sub_block, slot_start, per_panel, 2)
    row_slot = lax.dynamic_slice_in_dim(row_tile, slot_start, per_panel, 2)
    live_slot = lax.dynamic_slice_in_dim(present, slot_start, per_panel, 2) & has_col[:, :, None]
    owner_present = lax.dynamic_index_in_dim(present, my_col, 0, keepdims=False)
    owner_sets = lax.dynamic_index_in_dim(col_set, my_col, 0, keepdims=False)
    pick_rows = (mine_slot[..., None] & (sub_slot[..., None] == sub_range)).astype(jnp.bfloat16)
    rows_out = jnp.einsum(
        "ojps,sbw->opbw", pick_rows, row_blocks, preferred_element_type=jnp.float32
    ).astype(jnp.bfloat16)
    tiles_out = fock_tiles[row_slot, :, my_col_tile[:, :, None], :]
    tiles_out = jnp.where(live_slot[..., None, None], tiles_out, jnp.zeros_like(tiles_out))
    got_rows, got_tiles = (
        lax.all_to_all(rows_out, "col", split_axis=0, concat_axis=0, tiled=True),
        lax.all_to_all(tiles_out, "col", split_axis=0, concat_axis=0, tiled=True),
    )
    source = ((owner_sets[..., None] == set_range) & owner_present[..., None]).astype(jnp.bfloat16)
    source_slot = lax.dynamic_slice_in_dim(source, slot_start, per_panel, 1)
    source_slot = source_slot.reshape(num_panels, dev_lmos, per_panel, num_sets)
    strip_rows = jnp.einsum(
        "rdps,spbw->drpbw", source_slot, got_rows, preferred_element_type=jnp.float32
    ).astype(jnp.bfloat16)
    source_all = source.reshape(num_panels, dev_lmos, dom_blocks, num_sets)
    tiles_in = got_tiles.reshape(num_sets, num_panels, dev_lmos, per_panel, BLK, BLK)
    strip_fock = jnp.einsum(
        "rdks,srdpab->drpakb", source_all, tiles_in, preferred_element_type=jnp.float32
    ).astype(jnp.bfloat16)
    strip_fock = strip_fock.reshape(dev_lmos, num_panels, per_panel, BLK, dom_width)
    fin_rows, fin_fock = (
        lax.all_to_all(strip_rows, "row", split_axis=1, concat_axis=1, tiled=True),
        lax.all_to_all(strip_fock, "row", split_axis=1, concat_axis=1, tiled=True),
    )
    fin_rows = fin_rows.reshape(dev_lmos, dom_width, row_width)
    fin_fock = fin_fock.reshape(dev_lmos, dom_width, dom_width)
    slot_rot = rotation[0]
    coef_dom = fin_rows[:, :, :occ_width]
    proj_dom = fin_rows[:, :, occ_width : 2 * occ_width]
    three_dom = fin_rows[:, :, 2 * occ_width :]
    fock_half = jnp.einsum(
        "dxy,dyn->dxn", fin_fock, slot_rot, preferred_element_type=jnp.float32
    ).astype(jnp.bfloat16)
    fock_rot = jnp.einsum("dxm,dxn->dmn", slot_rot, fock_half, preferred_element_type=jnp.float32)
    coef_rot = jnp.einsum(
        "dxm,dxi->dmi", slot_rot, coef_dom, preferred_element_type=jnp.float32
    ).astype(jnp.bfloat16)
    proj_rot = jnp.einsum(
        "dxm,dxi->dmi", slot_rot, proj_dom, preferred_element_type=jnp.float32
    ).astype(jnp.bfloat16)
    proj_fock = fock_rot - jnp.einsum(
        "dmi,dni->dmn", coef_rot, proj_rot, preferred_element_type=jnp.float32
    )
    proj_fock = proj_fock - jnp.einsum(
        "dmi,dni->dmn", proj_rot, coef_rot, preferred_element_type=jnp.float32
    )
    three_rot = jnp.einsum(
        "dxm,dxu->dmu", slot_rot, three_dom, preferred_element_type=jnp.float32
    ).astype(jnp.bfloat16)
    return (proj_fock[None], three_rot[None])


def solution(mesh):
    placed = (
        P("row", "col", None),
        P(("row", "col"), None),
        P(("row", "col"), None),
        P("col", "row", None, None),
        P(),
        P(),
    )
    return jax.shard_map(
        body,
        mesh=mesh,
        in_specs=placed,
        out_specs=(P("col", "row", None, None), P("col", "row", None, None)),
        check_vma=False,
    )
```

profile of v0, /device:TPU:1, one launch (start us, length us, event | category | flops | bytes accessed | tf_op | source)
XLA Modules:
  0.0 609.3 jit_solution(9066787770218420429)
XLA Ops:
  7.2 0.7 all-gather.2.cloned.1.call-update
  8.0 37.6 %all-gather.2.cloned.1.call-done = bf16[2048,1024]{1,0:T(8,128)(2,1)} async-done(((bf16[256,1024]{1,0:T(8,128)(2,1)}), bf16[2048,1024]{1,0:T(8,128)(2,1)}) %all-gather.2.cloned.1.call-update) | async-done | bytes 4194320 | tf_op jit(solution)/shard_map/all_gather | solution.py:29
  45.5 23.4 %fusion.5 = bf16[4096,1024]{1,0:T(8,128)(2,1)} fusion(bf16[2048,1024]{1,0:T(8,128)(2,1)} %all-gather.2.cloned.1.call-done, bf16[4096,1,2048]{2,0,1:T(8,128)(2,1)} %param.6), kind=kOutput, calls=%fused_computation.8 | convolution fusion | flops 17184063488 | bytes 29360128 | tf_op jit(solution)/shard_map/dot_general | solution.py:31
  69.0 9.7 %copy.120 = bf16[512,8,16,128]{3,2,1,0:T(8,128)(2,1)S(1)} copy(bf16[512,8,16,128]{3,1,2,0:T(8,128)(2,1)} %bitcast.129) | data formatting | bytes 33554432
  78.6 8.1 %copy.94 = bf16[32,128,16,128]{3,1,2,0:T(8,128)(2,1)} copy(bf16[32,128,16,128]{3,2,1,0:T(8,128)(2,1)S(1)} %bitcast.127) | data formatting | bytes 33554432 | tf_op jit(solution)/shard_map/reshape;squeeze | solution.py:47
  86.8 0.1 copy.90
  86.9 0.1 copy.89
  87.0 0.1 reshape.164
  87.1 0.6 gather_fusion
  87.7 0.1 copy.91
  87.8 0.1 fusion.69
  87.9 0.1 add_select_fusion.1
  88.0 0.1 copy.93
  88.1 0.1 reshape.172
  88.2 0.1 copy.92
  88.3 9.6 %gather_fusion.1 = bf16[128,128,128]{2,1,0:T(8,128)(2,1)} fusion(bf16[32,128,16,128]{3,1,2,0:T(8,128)(2,1)} %copy.94, s32[128]{0:T(128)S(1)} %reshape.172), kind=kCustom, calls=%fused_computation.1 | custom fusion | bytes 8389632 | tf_op jit(solution)/shard_map/gather | solution.py:68
  97.8 4.6 select_bitcast_fusion
  102.4 6.9 %all-to-all-start = ((bf16[16,8,1,128,128]{4,3,1,2,0:T(8,128)(2,1)}), bf16[16,8,1,128,128]{4,3,1,2,0:T(8,128)(2,1)}, u32[]{:S(2)}, u32[]{:S(2)}) async-start(bf16[16,8,1,128,128]{4,3,1,2,0:T(8,128)(2,1)} %select_bitcast_fusion), calls=%async_computation | async-start | bytes 8388608 | tf_op jit(solution)/shard_map/all_to_all | solution.py:72
  109.3 92.5 %reduce-scatter.2.cloned.1.call-done = bf16[256,1024]{1,0:T(8,128)(2,1)} async-done(((bf16[4096,1024]{1,0:T(8,128)(2,1)}), bf16[256,1024]{1,0:T(8,128)(2,1)}) %reduce-scatter.2.cloned.1.call-update) | async-done | bytes 524304 | tf_op jit(solution)/shard_map/reduce_scatter | solution.py:30
  201.8 3.7 convolution_bitcast_fusion
  205.5 104.6 %all-reduce.1 = bf16[1024,1024]{0,1:T(8,128)(2,1)} all-reduce(f32[1024,1024]{0,1:T(8,128)} %convolution_bitcast_fusion), channel_id=1, replica_groups=mesh['row'=8,'col'=16] {'row','col'}, use_global_device_ids=true, to_apply=%region_4.5 | all-reduce | flops 1048576 | bytes 6291456 | tf_op jit(solution)/shard_map/psum | solution.py:39
  310.2 2.4 fusion.36
  312.6 0.1 pad_maximum_fusion
  312.7 5.9 convert_bitcast_fusion
  318.6 13.7 %copy.105 = bf16[16,1,128,2560]{3,2,1,0:T(8,128)(2,1)} copy(bf16[16,1,128,2560]{3,0,2,1:T(8,128)(2,1)} %convert_bitcast_fusion) | data formatting | bytes 20971520 | tf_op jit(solution)/shard_map/convert_element_type | solution.py:67
  332.3 5.2 all-to-all-start.2
  337.5 0.1 constant_dynamic-slice_fusion.1
  337.6 0.1 copy.116
  337.7 0.1 constant_dynamic-slice_fusion
  337.8 0.1 copy.117
  337.9 0.1 fusion.53
  338.0 4.6 convert_bitcast_fusion.1
  342.7 2.3 reshape.152
  345.0 144.6 %all-to-all-done.2 = bf16[16,1,128,2560]{3,2,1,0:T(8,128)(2,1)} async-done(((bf16[16,1,128,2560]{3,2,1,0:T(8,128)(2,1)}), bf16[16,1,128,2560]{3,2,1,0:T(8,128)(2,1)}, u32[]{:S(2)}, u32[]{:S(2)}) %all-to-all-start.2) | async-done | bytes 10485792 | tf_op jit(solution)/shard_map/all_to_all | solution.py:71
  489.5 9.3 %all-to-all-start.1 = ((bf16[1,8,1,128,1024]{4,3,2,0,1:T(8,128)(2,1)}), bf16[1,8,1,128,1024]{4,3,2,0,1:T(8,128)(2,1)S(1)}, u32[]{:S(2)}, u32[]{:S(2)}) async-start(bf16[1,8,1,128,1024]{4,3,2,0,1:T(8,128)(2,1)} %bitcast.16), calls=%async_computation.1 | async-start | bytes 4194304 | tf_op jit(solution)/shard_map/all_to_all | solution.py:88
  498.8 10.1 %fusion.11 = bf16[1,8,1,128,2560]{4,1,3,0,2:T(8,128)(2,1)S(1)} fusion(bf16[16,1,128,2560]{3,2,1,0:T(8,128)(2,1)} %all-to-all-done.2, pred[8,8,16]{2,0,1:T(8,128)(4,1)S(1)} %get-tuple-element.20, s32[]{:T(128)S(6)} %select_n.74), kind=kOutput, calls=%fused_computation.10 | convolution fusion | flops 86507520 | bytes 15729668 | tf_op jit(solution)/shard_map/rdps,spbw->drpbw/dot_general | solution.py:77
  508.9 3.8 copy.107
  512.8 12.4 %all-to-all-done.1 = bf16[1,8,1,128,1024]{4,3,2,0,1:T(8,128)(2,1)S(1)} async-done(((bf16[1,8,1,128,1024]{4,3,2,0,1:T(8,128)(2,1)}), bf16[1,8,1,128,1024]{4,3,2,0,1:T(8,128)(2,1)S(1)}, u32[]{:S(2)}, u32[]{:S(2)}) %all-to-all-start.1) | async-done | bytes 2097184 | tf_op jit(solution)/shard_map/all_to_all | solution.py:88
  525.2 5.4 all-to-all-start.3
  530.6 2.8 convolution_bitcast_fusion.1
  533.4 57.4 %all-to-all-done.3 = bf16[1,8,1,128,2560]{4,3,0,2,1:T(8,128)(2,1)} async-done(((bf16[1,8,1,128,2560]{4,3,0,2,1:T(8,128)(2,1)}), bf16[1,8,1,128,2560]{4,3,0,2,1:T(8,128)(2,1)}, u32[]{:S(2)}, u32[]{:S(2)}) %all-to-all-start.3) | async-done | bytes 5242912 | tf_op jit(solution)/shard_map/all_to_all | solution.py:87
  590.8 2.9 fusion.23
  593.6 2.9 fusion.24
  596.5 2.0 fusion.39
  598.6 0.8 convolution_subtract_fusion.1
  599.4 0.8 fusion.34
  600.1 1.3 copy.110
  601.4 1.0 copy.111
  (28 shorter events, 0.2 us)
Async XLA Ops:
  7.2 523.5 %copy-start = (bf16[1,1,1024,512]{3,2,1,0:T(8,128)(2,1)S(1)}, bf16[1,1,1024,512]{3,2,1,0:T(8,128)(2,1)}, u32[]{:S(2)}) copy-start(bf16[1,1,1024,512]{3,2,1,0:T(8,128)(2,1)} %param.9) | copy-start | bytes 3145732
  7.2 38.3 %all-gather.2.cloned.1.call-start = ((), (), s32[]{:S(2)}) async-start(), calls=%async_computation.5 | async-start | bytes 4718592 | tf_op jit(solution)/shard_map/all_gather | solution.py:29
  7.9 193.9 %reduce-scatter.2.cloned.1.call-start = ((), (), s32[]{:S(2)}) async-start(), calls=%async_computation.6 | async-start | bytes 8912896 | tf_op jit(solution)/shard_map/reduce_scatter | solution.py:30
  78.6 8.2 %copy-start.6 = (s32[128,8]{0,1:T(8,128)S(1)}, s32[128,8]{0,1:T(8,128)}, u32[]{:S(2)}) copy-start(s32[128,8]{0,1:T(8,128)} %param.11) | copy-start | bytes 12292
  78.6 8.3 %copy-start.5 = (s32[16,8]{0,1:T(8,128)S(1)}, s32[16,8]{0,1:T(8,128)}, u32[]{:S(2)}) copy-start(s32[16,8]{0,1:T(8,128)} %param.10) | copy-start | bytes 1540
  102.4 99.4 %copy-start.1 = (bf16[256,1024]{1,0:T(8,128)(2,1)S(1)}, bf16[256,1024]{1,0:T(8,128)(2,1)}, u32[]{:S(2)}) copy-start(bf16[256,1024]{1,0:T(8,128)(2,1)} %param.7) | copy-start | bytes 1572868
  102.4 229.9 %all-to-all-start = ((bf16[16,8,1,128,128]{4,3,1,2,0:T(8,128)(2,1)}), bf16[16,8,1,128,128]{4,3,1,2,0:T(8,128)(2,1)}, u32[]{:S(2)}, u32[]{:S(2)}) async-start(bf16[16,8,1,128,128]{4,3,1,2,0:T(8,128)(2,1)} %select_bitcast_fusion), calls=%async_computation | async-start | bytes 8388608 | tf_op jit(solution)/shard_map/all_to_all | solution.py:72
  205.5 104.7 %copy-start.2 = (bf16[256,1024]{1,0:T(8,128)(2,1)S(1)}, bf16[256,1024]{1,0:T(8,128)(2,1)}, u32[]{:S(2)}) copy-start(bf16[256,1024]{1,0:T(8,128)(2,1)} %reduce-scatter.2.cloned.1.call-done) | copy-start | bytes 1572868
  310.2 2.4 copy-start.4
  332.3 157.2 %all-to-all-start.2 = ((bf16[16,1,128,2560]{3,2,1,0:T(8,128)(2,1)}), bf16[16,1,128,2560]{3,2,1,0:T(8,128)(2,1)}, u32[]{:S(2)}, u32[]{:S(2)}) async-start(bf16[16,1,128,2560]{3,2,1,0:T(8,128)(2,1)} %copy.105), calls=%async_computation.3 | async-start | bytes 20971520 | tf_op jit(solution)/shard_map/all_to_all | solution.py:71
  489.5 35.7 %all-to-all-start.1 = ((bf16[1,8,1,128,1024]{4,3,2,0,1:T(8,128)(2,1)}), bf16[1,8,1,128,1024]{4,3,2,0,1:T(8,128)(2,1)S(1)}, u32[]{:S(2)}, u32[]{:S(2)}) async-start(bf16[1,8,1,128,1024]{4,3,2,0,1:T(8,128)(2,1)} %bitcast.16), calls=%async_computation.1 | async-start | bytes 4194304 | tf_op jit(solution)/shard_map/all_to_all | solution.py:88
  525.2 65.6 %all-to-all-start.3 = ((bf16[1,8,1,128,2560]{4,3,0,2,1:T(8,128)(2,1)}), bf16[1,8,1,128,2560]{4,3,0,2,1:T(8,128)(2,1)}, u32[]{:S(2)}, u32[]{:S(2)}) async-start(bf16[1,8,1,128,2560]{4,3,0,2,1:T(8,128)(2,1)} %copy.107), calls=%async_computation.4 | async-start | bytes 10485760 | tf_op jit(solution)/shard_map/all_to_all | solution.py:87
  596.5 2.1 copy-start.3
Sparse Core Ops, SparseCore 0:
  9.7 35.7 all-gather.1
  69.1 132.6 reduce-scatter.1
where the time goes:
time: 610 us; the launch traced here: 609 us
  waiting for transfers between devices  345 us (57%)
  blocking collectives  105 us (17%)
  matrix products  62.2 us (10%)
  local copies, waits for them, and re-layouts  51.2 us (8%)
  starting transfers between devices  26.9 us (4%)
  between operations  14.3 us (2%)
    all_to_all x1, waiting for transfers between devices, body(): lax.all_to_all(rows_out, 'col', split_axis=0, concat_axis=0, tiled=True)  145 us
    psum x1, blocking collectives, body(): occ_fock = lax.psum(occ_term, ('row', 'col'))  105 us
    reduce_scatter x1, waiting for transfers between devices, body(): lax.psum_scatter(jnp.dot(panel_fock, gathered, preferred_element_type=jnp...  92.5 us
    all_to_all x1, waiting for transfers between devices, body(): lax.all_to_all(strip_rows, 'row', split_axis=1, concat_axis=1, tiled=True)  57.4 us
    all_gather x1, waiting for transfers between devices, body(): gathered = lax.all_gather(lmo_coef, 'row', axis=0, tiled=True)  37.6 us
    dot_general x1, matrix products, body(): jnp.dot(panel_fock, gathered, preferred_element_type=jnp.float32)  23.4 us
    convert_element_type x1, local copies, waits for them, and re-layouts, body(): rows_out = jnp.einsum('ojps,sbw->opbw', pick_rows, row_blocks, preferred_...  13.7 us
    all_to_all x1, waiting for transfers between devices, body(): lax.all_to_all(strip_fock, 'row', split_axis=1, concat_axis=1, tiled=True)  12.4 us
  transfers between devices with their start and end apart: 6, of which 5 were waited for; matrix products, arithmetic and copies ran while one was open for 14% of the time, Pallas kernels for 0%

commit v1 on v0

--- a/solution.py
+++ b/solution.py
@@ -4,6 +4,11 @@
 from jax.sharding import PartitionSpec as P
 
 BLK = 128
+
+
+def gather_over(shard, mesh_axis, dim):
+    sent = jnp.stack([shard] * lax.axis_size(mesh_axis))
+    return jnp.concatenate(lax.all_to_all(sent, mesh_axis, 0, 0), axis=dim)
 
 
 def locate(blocks, dev_blocks, num_sets):
@@ -26,7 +31,7 @@
     dev_lmos = rotation.shape[1]
     dom_width = dom_blocks * BLK
     panel_fock = fock[:, 0, :]
-    gathered = lax.all_gather(lmo_coef, "row", axis=0, tiled=True)
+    gathered = gather_over(lmo_coef, "row", 0)
     fock_coef = lax.psum_scatter(
         jnp.dot(panel_fock, gathered, preferred_element_type=jnp.float32).astype(jnp.bfloat16),
         "col",

time: 610 us -> 638 us (1.046); the launches traced: 609 us -> 630 us
  blocking collectives: 105 us -> 160 us
  waiting for transfers between devices: 345 us -> 308 us
    all_to_all x0 -> x1, blocking collectives: none -> 55.1 us  [gather_over(): return jnp.concatenate(lax.all_to_all(sent, mesh_axis, 0, 0), axis=dim)]
    all_gather x1 -> x0, waiting for transfers between devices: 37.6 us -> none  [body(): gathered = lax.all_gather(lmo_coef, 'row', axis=0, tiled=True)]
  transfers between devices with their start and end apart: 6 -> 5, of which waited for: 5 -> 4; matrix products, arithmetic and copies ran while one was open for 14% -> 13% of each run, Pallas kernels for 0% -> 0%
where the time goes in v1:
time: 638 us; the launch traced here: 630 us
  waiting for transfers between devices  308 us (48%)
  blocking collectives  160 us (25%)
  matrix products  61 us (10%)
  local copies, waits for them, and re-layouts  52.9 us (8%)
  starting transfers between devices  29.1 us (5%)
  between operations  14.5 us (2%)
    all_to_all x1, waiting for transfers between devices, body(): lax.all_to_all(rows_out, 'col', split_axis=0, concat_axis=0, tiled=True)  144 us
    psum x1, blocking collectives, body(): occ_fock = lax.psum(occ_term, ('row', 'col'))  105 us
    reduce_scatter x1, waiting for transfers between devices, body(): lax.psum_scatter(jnp.dot(panel_fock, gathered, preferred_element_type=jnp...  94.1 us
    all_to_all x1, waiting for transfers between devices, body(): lax.all_to_all(strip_rows, 'row', split_axis=1, concat_axis=1, tiled=True)  57.3 us
    all_to_all x1, blocking collectives, gather_over(): return jnp.concatenate(lax.all_to_all(sent, mesh_axis, 0, 0), axis=dim)  55.1 us
    dot_general x1, matrix products, body(): jnp.dot(panel_fock, gathered, preferred_element_type=jnp.float32)  22.2 us
    convert_element_type x1, local copies, waits for them, and re-layouts, body(): rows_out = jnp.einsum('ojps,sbw->opbw', pick_rows, row_blocks, preferred_...  13.7 us
  transfers between devices with their start and end apart: 5, of which 4 were waited for; matrix products, arithmetic and copies ran while one was open for 13% of the time, Pallas kernels for 0%

profile of v1, /device:TPU:1, one launch (start us, length us, event | category | flops | bytes accessed | tf_op | source)
XLA Modules:
  0.0 630.4 jit_solution(10556257890780856384)
XLA Ops:
  7.2 1.6 stack.2
  8.9 55.1 %all_to_all.25 = bf16[8,256,1024]{2,1,0:T(8,128)(2,1)S(1)} all-to-all(bf16[8,256,1024]{2,1,0:T(8,128)(2,1)S(1)} %stack.2), channel_id=1, replica_groups=mesh['row'=8,'col'=16] {'row'}, dimensions={0} | all-to-all | bytes 8388608 | tf_op jit(solution)/shard_map/all_to_all | solution.py:11
  63.9 22.2 %fusion.5 = bf16[4096,1024]{1,0:T(8,128)(2,1)} fusion(bf16[2048,1024]{1,0:T(8,128)(2,1)S(1)} %bitcast.132, bf16[4096,1,2048]{2,0,1:T(8,128)(2,1)} %param.6), kind=kOutput, calls=%fused_computation.8 | convolution fusion | flops 17184063488 | bytes 29360128 | tf_op jit(solution)/shard_map/dot_general | solution.py:36
  86.1 9.7 %copy.120 = bf16[512,8,16,128]{3,2,1,0:T(8,128)(2,1)S(1)} copy(bf16[512,8,16,128]{3,1,2,0:T(8,128)(2,1)} %bitcast.130) | data formatting | bytes 33554432
  95.8 8.2 %copy.94 = bf16[32,128,16,128]{3,1,2,0:T(8,128)(2,1)} copy(bf16[32,128,16,128]{3,2,1,0:T(8,128)(2,1)S(1)} %bitcast.128) | data formatting | bytes 33554432 | tf_op jit(solution)/shard_map/reshape;squeeze | solution.py:52
  104.0 0.1 copy.90
  104.1 0.1 copy.89
  104.2 0.1 reshape.170
  104.3 0.6 gather_fusion
  104.9 0.1 copy.91
  105.0 0.1 fusion.69
  105.1 0.1 add_select_fusion.1
  105.2 0.1 copy.93
  105.3 0.1 reshape.178
  105.4 0.1 copy.92
  105.5 9.6 %gather_fusion.1 = bf16[128,128,128]{2,1,0:T(8,128)(2,1)} fusion(bf16[32,128,16,128]{3,1,2,0:T(8,128)(2,1)} %copy.94, s32[128]{0:T(128)S(1)} %reshape.178), kind=kCustom, calls=%fused_computation.1 | custom fusion | bytes 8389632 | tf_op jit(solution)/shard_map/gather | solution.py:73
  115.1 4.5 select_bitcast_fusion
  119.6 7.7 %all-to-all-start = ((bf16[16,8,1,128,128]{4,3,1,2,0:T(8,128)(2,1)}), bf16[16,8,1,128,128]{4,3,1,2,0:T(8,128)(2,1)}, u32[]{:S(2)}, u32[]{:S(2)}) async-start(bf16[16,8,1,128,128]{4,3,1,2,0:T(8,128)(2,1)} %select_bitcast_fusion), calls=%async_computation | async-start | bytes 8388608 | tf_op jit(solution)/shard_map/all_to_all | solution.py:77
  127.4 94.1 %reduce-scatter.2.cloned.1.call-done = bf16[256,1024]{1,0:T(8,128)(2,1)} async-done(((bf16[4096,1024]{1,0:T(8,128)(2,1)}), bf16[256,1024]{1,0:T(8,128)(2,1)}) %reduce-scatter.2.cloned.1.call-update) | async-done | bytes 524304 | tf_op jit(solution)/shard_map/reduce_scatter | solution.py:35
  221.5 3.7 convolution_bitcast_fusion
  225.2 104.6 %all-reduce.1 = bf16[1024,1024]{0,1:T(8,128)(2,1)} all-reduce(f32[1024,1024]{0,1:T(8,128)} %convolution_bitcast_fusion), channel_id=1, replica_groups=mesh['row'=8,'col'=16] {'row','col'}, use_global_device_ids=true, to_apply=%region_4.5 | all-reduce | flops 1048576 | bytes 6291456 | tf_op jit(solution)/shard_map/psum | solution.py:44
  329.8 2.4 fusion.36
  332.2 0.1 pad_maximum_fusion
  332.3 5.9 convert_bitcast_fusion
  338.2 13.7 %copy.105 = bf16[16,1,128,2560]{3,2,1,0:T(8,128)(2,1)} copy(bf16[16,1,128,2560]{3,0,2,1:T(8,128)(2,1)} %convert_bitcast_fusion) | data formatting | bytes 20971520 | tf_op jit(solution)/shard_map/convert_element_type | solution.py:72
  351.9 5.7 all-to-all-start.3
  357.7 0.1 constant_dynamic-slice_fusion.1
  357.8 0.1 copy.116
  357.9 0.1 constant_dynamic-slice_fusion
  358.0 0.1 copy.117
  358.1 0.1 fusion.53
  358.2 4.6 convert_bitcast_fusion.1
  362.8 2.3 reshape.157
  365.1 144.5 %all-to-all-done.3 = bf16[16,1,128,2560]{3,2,1,0:T(8,128)(2,1)} async-done(((bf16[16,1,128,2560]{3,2,1,0:T(8,128)(2,1)}), bf16[16,1,128,2560]{3,2,1,0:T(8,128)(2,1)}, u32[]{:S(2)}, u32[]{:S(2)}) %all-to-all-start.3) | async-done | bytes 10485792 | tf_op jit(solution)/shard_map/all_to_all | solution.py:76
  509.6 10.0 %all-to-all-start.1 = ((bf16[1,8,1,128,1024]{4,3,2,0,1:T(8,128)(2,1)}), bf16[1,8,1,128,1024]{4,3,2,0,1:T(8,128)(2,1)S(1)}, u32[]{:S(2)}, u32[]{:S(2)}) async-start(bf16[1,8,1,128,1024]{4,3,2,0,1:T(8,128)(2,1)} %bitcast.16), calls=%async_computation.1 | async-start | bytes 4194304 | tf_op jit(solution)/shard_map/all_to_all | solution.py:93
  519.6 10.1 %fusion.11 = bf16[1,8,1,128,2560]{4,1,3,0,2:T(8,128)(2,1)S(1)} fusion(bf16[16,1,128,2560]{3,2,1,0:T(8,128)(2,1)} %all-to-all-done.3, pred[8,8,16]{2,0,1:T(8,128)(4,1)S(1)} %get-tuple-element.20, s32[]{:T(128)S(6)} %select_n.74), kind=kOutput, calls=%fused_computation.10 | convolution fusion | flops 86507520 | bytes 15729668 | tf_op jit(solution)/shard_map/rdps,spbw->drpbw/dot_general | solution.py:82
  529.6 3.8 copy.107
  533.5 12.4 %all-to-all-done.1 = bf16[1,8,1,128,1024]{4,3,2,0,1:T(8,128)(2,1)S(1)} async-done(((bf16[1,8,1,128,1024]{4,3,2,0,1:T(8,128)(2,1)}), bf16[1,8,1,128,1024]{4,3,2,0,1:T(8,128)(2,1)S(1)}, u32[]{:S(2)}, u32[]{:S(2)}) %all-to-all-start.1) | async-done | bytes 2097184 | tf_op jit(solution)/shard_map/all_to_all | solution.py:93
  545.9 5.7 all-to-all-start.4
  551.6 2.8 convolution_bitcast_fusion.1
  554.3 57.3 %all-to-all-done.4 = bf16[1,8,1,128,2560]{4,3,0,2,1:T(8,128)(2,1)} async-done(((bf16[1,8,1,128,2560]{4,3,0,2,1:T(8,128)(2,1)}), bf16[1,8,1,128,2560]{4,3,0,2,1:T(8,128)(2,1)}, u32[]{:S(2)}, u32[]{:S(2)}) %all-to-all-start.4) | async-done | bytes 5242912 | tf_op jit(solution)/shard_map/all_to_all | solution.py:92
  611.6 2.9 fusion.23
  614.5 2.9 fusion.24
  617.4 2.0 fusion.39
  619.5 0.8 convolution_subtract_fusion.1
  620.2 0.8 fusion.34
  621.0 1.3 copy.110
  622.3 1.0 copy.111
  (27 shorter events, 0.2 us)
Async XLA Ops:
  7.2 544.4 %copy-start = (bf16[1,1,1024,512]{3,2,1,0:T(8,128)(2,1)S(1)}, bf16[1,1,1024,512]{3,2,1,0:T(8,128)(2,1)}, u32[]{:S(2)}) copy-start(bf16[1,1,1024,512]{3,2,1,0:T(8,128)(2,1)} %param.9) | copy-start | bytes 3145732
  7.2 214.3 %reduce-scatter.2.cloned.1.call-start = ((), (), s32[]{:S(2)}) async-start(), calls=%async_computation.6 | async-start | bytes 8912896 | tf_op jit(solution)/shard_map/reduce_scatter | solution.py:35
  95.8 8.2 %copy-start.6 = (s32[128,8]{0,1:T(8,128)S(1)}, s32[128,8]{0,1:T(8,128)}, u32[]{:S(2)}) copy-start(s32[128,8]{0,1:T(8,128)} %param.11) | copy-start | bytes 12292
  95.8 8.3 %copy-start.5 = (s32[16,8]{0,1:T(8,128)S(1)}, s32[16,8]{0,1:T(8,128)}, u32[]{:S(2)}) copy-start(s32[16,8]{0,1:T(8,128)} %param.10) | copy-start | bytes 1540
  119.6 101.9 %copy-start.1 = (bf16[256,1024]{1,0:T(8,128)(2,1)S(1)}, bf16[256,1024]{1,0:T(8,128)(2,1)}, u32[]{:S(2)}) copy-start(bf16[256,1024]{1,0:T(8,128)(2,1)} %param.7) | copy-start | bytes 1572868
  119.6 232.3 %all-to-all-start = ((bf16[16,8,1,128,128]{4,3,1,2,0:T(8,128)(2,1)}), bf16[16,8,1,128,128]{4,3,1,2,0:T(8,128)(2,1)}, u32[]{:S(2)}, u32[]{:S(2)}) async-start(bf16[16,8,1,128,128]{4,3,1,2,0:T(8,128)(2,1)} %select_bitcast_fusion), calls=%async_computation | async-start | bytes 8388608 | tf_op jit(solution)/shard_map/all_to_all | solution.py:77
  225.2 104.6 %copy-start.2 = (bf16[256,1024]{1,0:T(8,128)(2,1)S(1)}, bf16[256,1024]{1,0:T(8,128)(2,1)}, u32[]{:S(2)}) copy-start(bf16[256,1024]{1,0:T(8,128)(2,1)} %reduce-scatter.2.cloned.1.call-done) | copy-start | bytes 1572868
  329.8 2.4 copy-start.4
  351.9 157.6 %all-to-all-start.3 = ((bf16[16,1,128,2560]{3,2,1,0:T(8,128)(2,1)}), bf16[16,1,128,2560]{3,2,1,0:T(8,128)(2,1)}, u32[]{:S(2)}, u32[]{:S(2)}) async-start(bf16[16,1,128,2560]{3,2,1,0:T(8,128)(2,1)} %copy.105), calls=%async_computation.4 | async-start | bytes 20971520 | tf_op jit(solution)/shard_map/all_to_all | solution.py:76
  509.6 36.3 %all-to-all-start.1 = ((bf16[1,8,1,128,1024]{4,3,2,0,1:T(8,128)(2,1)}), bf16[1,8,1,128,1024]{4,3,2,0,1:T(8,128)(2,1)S(1)}, u32[]{:S(2)}, u32[]{:S(2)}) async-start(bf16[1,8,1,128,1024]{4,3,2,0,1:T(8,128)(2,1)} %bitcast.16), calls=%async_computation.1 | async-start | bytes 4194304 | tf_op jit(solution)/shard_map/all_to_all | solution.py:93
  545.9 65.8 %all-to-all-start.4 = ((bf16[1,8,1,128,2560]{4,3,0,2,1:T(8,128)(2,1)}), bf16[1,8,1,128,2560]{4,3,0,2,1:T(8,128)(2,1)}, u32[]{:S(2)}, u32[]{:S(2)}) async-start(bf16[1,8,1,128,2560]{4,3,0,2,1:T(8,128)(2,1)} %copy.107), calls=%async_computation.5 | async-start | bytes 10485760 | tf_op jit(solution)/shard_map/all_to_all | solution.py:92
  617.4 2.1 copy-start.3
Sparse Core Ops, SparseCore 0:
  86.3 135.1 reduce-scatter.1
